TPU v7x, 256 devices: a whole 4x4x8 slice. The times are simulated.
256 devices in a mesh: dp: 64 (over y, z, core), mp: 4 (over x).
Axes of the slice: x: 4, y: 4, z: 8, core: 2. Of those that a mesh axis runs over, the one named last changes fastest.
Arguments:
- queries: bfloat16 [32768, 1024], P('dp', 'mp'), may hold values from -20 to 20
- passages: bfloat16 [262144, 1024], P('dp', 'mp'), may hold values from -6 to 6
- positives: int32 [32768], P('dp'), may hold values from 0 to 4095, as said below
- negatives: int32 [64, 64], replicated, may hold values from -1 to 31, as said below
Outputs:
- losses: float32 [32768], P('dp')
- query_grad: float32 [32768, 1024], P('dp', 'mp')
- passage_grad: float32 [262144, 1024], P('dp', 'mp')
Inputs may be any that keep to these rules, and one draw needn't show every extreme that they name: Within each dp index the 512 positives of its query block are distinct. `negatives`: each row names between 16 and 64 blocks (entries >= 0); some row names 64.
All inputs are finite; a program needn't handle non-finite values.
Results may differ from a plain program's by a relative error of at most 0.0075.
Values may be sent and summed in bfloat16 or wider, within the bound.
No kernel may reach another device: no remote copies, remote signals or barrier semaphores. Data moves between devices by JAX's collectives and lax.ppermute only.
A program may use at most 128 MiB of HBM per device.

v0:
```python
import jax
import jax.numpy as jnp
from jax import lax
from jax.sharding import PartitionSpec as P

PBS = 128
HALVES = 2


def body(queries, passages, positives, negatives):
    dp_count = lax.axis_size("dp")
    mp_count = lax.axis_size("mp")
    own_index = lax.axis_index("dp")
    width_index = lax.axis_index("mp")
    query_rows, shard_width = queries.shape
    factor = (shard_width * mp_count) ** (-0.5)
    block_count = passages.shape[0] // PBS
    slots_per = dp_count // mp_count
    pos_per = query_rows // mp_count
    part = PBS // HALVES
    blocks = passages.reshape(block_count, PBS, shard_width)
    asked = lax.dynamic_index_in_dim(negatives, own_index, 1, keepdims=False)
    outgoing = jnp.take(blocks, jnp.maximum(asked, 0), axis=0)
    outgoing = jnp.where((asked >= 0)[:, None, None], outgoing, jnp.zeros_like(outgoing))
    wanted = lax.dynamic_index_in_dim(negatives, own_index, 0, keepdims=False)
    my_slots = lax.dynamic_slice_in_dim(wanted, width_index * slots_per, slots_per) >= 0
    q_full = lax.all_gather(queries, "mp", axis=1, tiled=True)
    q4 = q_full.reshape(query_rows, mp_count, shard_width)
    positive_rows = jnp.take(passages, positives, axis=0)
    mine, valid = ([], [])
    for h in range(HALVES):
        fetched = lax.all_to_all(
            outgoing[:, h * part : (h + 1) * part], "dp", split_axis=0, concat_axis=0, tiled=True
        )
        send = fetched.reshape(mp_count, slots_per * part, shard_width)
        ok = jnp.broadcast_to(my_slots[:, None], (slots_per, part)).reshape(-1)
        if h == 0:
            send = jnp.concatenate(
                [positive_rows.reshape(mp_count, pos_per, shard_width), send], axis=1
            )
            ok = jnp.concatenate([jnp.ones((pos_per,), bool), ok])
        mine.append(lax.all_to_all(send, "mp", split_axis=0, concat_axis=0, tiled=True))
        valid.append(ok)
    scores = [
        factor
        * lax.dot_general(c, q4, (((0, 2), (1, 2)), ((), ())), preferred_element_type=jnp.float32)
        for c in mine
    ]
    masked = [jnp.where(v[:, None], s, jnp.float32(-1e30)) for s, v in zip(scores, valid)]
    local_top = jnp.max(jnp.stack([jnp.max(x, axis=0) for x in masked]), axis=0)
    local_total = sum(
        (
            jnp.sum(jnp.where(v[:, None], jnp.exp(x - local_top), jnp.float32(0.0)), axis=0)
            for x, v in zip(masked, valid)
        )
    )
    target = (width_index * pos_per + jnp.arange(pos_per, dtype=jnp.int32))[:, None] == jnp.arange(
        query_rows, dtype=jnp.int32
    )[None, :]
    local_own = jnp.sum(jnp.where(target, scores[0][:pos_per], jnp.float32(0.0)), axis=0)
    stats = lax.all_gather(jnp.stack([local_top, local_total, local_own]), "mp", axis=0)
    top = jnp.max(stats[:, 0], axis=0)
    total = jnp.sum(stats[:, 1] * jnp.exp(stats[:, 0] - top), axis=0)
    own_score = jnp.sum(stats[:, 2], axis=0)
    lse = top + jnp.log(total)
    losses = lse - own_score
    grads = []
    for h in range(HALVES):
        prob = jnp.where(valid[h][:, None], jnp.exp(masked[h] - lse), jnp.float32(0.0))
        if h == 0:
            prob = jnp.concatenate([prob[:pos_per] - target.astype(jnp.float32), prob[pos_per:]])
        grads.append(prob.astype(jnp.bfloat16))
    query_part = sum(
        (
            lax.dot_general(g, c, (((0,), (1,)), ((), ())), preferred_element_type=jnp.float32)
            for g, c in zip(grads, mine)
        )
    )
    query_grad = lax.psum_scatter(factor * query_part, "mp", scatter_dimension=1, tiled=True)
    query_grad = query_grad.reshape(query_rows, shard_width)
    returned, pos_back = ([], None)
    for h in range(HALVES):
        cand = factor * jnp.dot(grads[h], q_full, preferred_element_type=jnp.float32)
        rows = cand.shape[0]
        pieces = []
        if h == 0:
            pos = cand[:pos_per]
            rounded = lax.reduce_precision(pos, exponent_bits=8, mantissa_bits=7)
            high = rounded.astype(jnp.bfloat16)
            low = (pos - rounded).astype(jnp.bfloat16)
            for x in (high, low):
                pieces.append(x.reshape(pos_per, mp_count, shard_width).transpose(1, 0, 2))
            cand = cand[pos_per:]
            rows -= pos_per
        neg = cand.astype(jnp.bfloat16).reshape(rows, mp_count, shard_width).transpose(1, 0, 2)
        pieces.append(neg)
        sent = lax.all_to_all(
            jnp.concatenate(pieces, axis=1), "mp", split_axis=0, concat_axis=0, tiled=True
        )
        if h == 0:
            pos_back = (
                sent[:, :pos_per].astype(jnp.float32)
                + sent[:, pos_per : 2 * pos_per].astype(jnp.float32)
            ).reshape(query_rows, shard_width)
            sent = sent[:, 2 * pos_per :]
        back = lax.all_to_all(
            sent.reshape(dp_count, part, shard_width), "dp", split_axis=0, concat_axis=0, tiled=True
        )
        returned.append(back)
    returned = jnp.concatenate(returned, axis=1).astype(jnp.float32)
    selector = (asked[None, :] == jnp.arange(block_count, dtype=jnp.int32)[:, None]).astype(
        jnp.float32
    )
    block_grad = jnp.einsum("kr,rpd->kpd", selector, returned, precision=lax.Precision.HIGHEST)
    passage_grad = block_grad.reshape(block_count * PBS, shard_width).at[positives].add(pos_back)
    return (losses, query_grad, passage_grad)


def solution(mesh):
    in_specs = (P("dp", "mp"), P("dp", "mp"), P("dp"), P())
    out_specs = (P("dp"), P("dp", "mp"), P("dp", "mp"))
    return jax.shard_map(body, mesh=mesh, in_specs=in_specs, out_specs=out_specs, check_vma=False)
```

profile of v0, /device:TPU:1, one launch (start us, length us, event | category | flops | bytes accessed | tf_op | source)
XLA Modules:
  0.0 430.8 jit_solution(1757947262718900918)
XLA Ops:
  7.2 1.1 dynamic-slice_reduce_fusion
  8.3 0.9 compare_reduce_fusion
  9.3 2.8 gather_fusion.1
  12.1 2.7 select_select_fusion
  14.8 0.6 fusion.23
  15.3 64.3 %all_to_all.40 = bf16[64,64,256]{2,1,0:T(8,128)(2,1)} all-to-all(bf16[64,64,256]{2,1,0:T(8,128)(2,1)S(1)} %get-tuple-element.12), channel_id=1, replica_groups=mesh['dp'=64,'mp'=4] {'dp'}, dimensions={0} | all-to-all | bytes 4194304 | tf_op jit(solution)/shard_map/all_to_all | solution.py:32
  79.7 57.0 %all_to_all.41 = bf16[64,64,256]{2,1,0:T(8,128)(2,1)} all-to-all(bf16[64,64,256]{2,1,0:T(8,128)(2,1)S(1)} %get-tuple-element.11), channel_id=1, replica_groups=mesh['dp'=64,'mp'=4] {'dp'}, dimensions={0} | all-to-all | bytes 4194304 | tf_op jit(solution)/shard_map/all_to_all | solution.py:32
  136.6 4.6 %all-to-all-start.3 = ((bf16[4,1024,256]{2,1,0:T(8,128)(2,1)}), bf16[4,1024,256]{2,1,0:T(8,128)(2,1)}, u32[]{:S(2)}, u32[]{:S(2)}) async-start(bf16[4,1024,256]{2,1,0:T(8,128)(2,1)} %bitcast.68), calls=%async_computation.3 | async-start | bytes 4194304 | tf_op jit(solution)/shard_map/all_to_all | solution.py:42
  141.3 0.8 copy.24
  142.2 2.0 gather_fusion
  144.3 3.2 pad_maximum_fusion.1
  147.4 28.3 %all-to-all-done.3 = bf16[4,1024,256]{2,1,0:T(8,128)(2,1)} async-done(((bf16[4,1024,256]{2,1,0:T(8,128)(2,1)}), bf16[4,1024,256]{2,1,0:T(8,128)(2,1)}, u32[]{:S(2)}, u32[]{:S(2)}) %all-to-all-start.3) | async-done | bytes 2097184 | tf_op jit(solution)/shard_map/all_to_all | solution.py:42
  175.7 4.5 %all-to-all-start.1 = ((bf16[4,1152,256]{2,1,0:T(8,128)(2,1)}), bf16[4,1152,256]{2,1,0:T(8,128)(2,1)}, u32[]{:S(2)}, u32[]{:S(2)}) async-start(bf16[4,1152,256]{2,1,0:T(8,128)(2,1)} %pad_maximum_fusion.1), calls=%async_computation.1 | async-start | bytes 4718592 | tf_op jit(solution)/shard_map/all_to_all | solution.py:42
  180.3 0.8 compare_bitcast_fusion
  181.2 3.1 fusion.25
  184.4 23.9 %all-to-all-done.1 = bf16[4,1152,256]{2,1,0:T(8,128)(2,1)} async-done(((bf16[4,1152,256]{2,1,0:T(8,128)(2,1)}), bf16[4,1152,256]{2,1,0:T(8,128)(2,1)}, u32[]{:S(2)}, u32[]{:S(2)}) %all-to-all-start.1) | async-done | bytes 2359328 | tf_op jit(solution)/shard_map/all_to_all | solution.py:42
  208.3 3.4 select_reduce_fusion.2
  211.8 0.6 select_reduce_fusion
  212.3 0.4 select_reduce_fusion.1
  213.0 9.1 %all-gather.1 = f32[4,3,512]{2,1,0:T(4,128)S(1)} all-gather(f32[1,3,512]{2,1,0:T(4,128)S(1)} %maximum_bitcast_fusion), channel_id=2, replica_groups=mesh['dp'=64,'mp'=4] {'mp'}, dimensions={0}, use_global_device_ids=true | all-gather | bytes 30720 | tf_op jit(solution)/shard_map/all_gather | solution.py:61
  222.2 0.6 fusion.22
  222.8 2.8 multiply_convert_fusion
  225.6 4.0 copy.33
  229.6 4.6 %all-to-all-start.6 = ((bf16[4,1024,256]{2,1,0:T(8,128)(2,1)}), bf16[4,1024,256]{2,1,0:T(8,128)(2,1)}, u32[]{:S(2)}, u32[]{:S(2)}) async-start(bf16[4,1024,256]{2,1,0:T(8,128)(2,1)} %bitcast.26), calls=%async_computation.7 | async-start | bytes 4194304 | tf_op jit(solution)/shard_map/all_to_all | solution.py:97
  234.2 2.1 exponential_select_fusion
  236.7 0.9 copy-done.7
  237.5 0.4 copy-done.12
  238.0 1.6 convolution_multiply_fusion
  239.6 1.9 slice.86
  241.5 0.9 copy-done.6
  242.3 2.8 copy.32
  245.2 1.1 reduce-precision_convert_fusion
  246.6 1.7 pad_maximum_fusion
  248.3 7.3 %all-to-all-done.6 = bf16[4,1024,256]{2,1,0:T(8,128)(2,1)} async-done(((bf16[4,1024,256]{2,1,0:T(8,128)(2,1)}), bf16[4,1024,256]{2,1,0:T(8,128)(2,1)}, u32[]{:S(2)}, u32[]{:S(2)}) %all-to-all-start.6) | async-done | bytes 2097184 | tf_op jit(solution)/shard_map/all_to_all | solution.py:97
  255.6 30.6 %all_to_all.42 = bf16[4,1280,256]{2,1,0:T(8,128)(2,1)} all-to-all(bf16[4,1280,256]{2,1,0:T(8,128)(2,1)} %pad_maximum_fusion), channel_id=1, replica_groups=mesh['dp'=64,'mp'=4] {'mp'}, dimensions={0} | all-to-all | bytes 5242880 | tf_op jit(solution)/shard_map/all_to_all | solution.py:97
  286.2 14.0 %all-to-all-start.7 = ((bf16[64,64,256]{2,1,0:T(8,128)(2,1)}), bf16[64,64,256]{2,1,0:T(8,128)(2,1)S(1)}, u32[]{:S(2)}, u32[]{:S(2)}) async-start(bf16[64,64,256]{2,1,0:T(8,128)(2,1)} %bitcast.27), calls=%async_computation.8 | async-start | bytes 4194304 | tf_op jit(solution)/shard_map/all_to_all | solution.py:106
  300.2 5.1 %fusion.7 = f32[512,4,256]{2,0,1:T(8,128)} fusion(bf16[4,1024,256]{2,1,0:T(8,128)(2,1)} %all-to-all-done.3, f32[1024,512]{1,0:T(8,128)} %copy-done.5, f32[512]{0:T(512)S(1)} %get-tuple-element.8, pred[1024]{0:T(1024)(128)(4,1)S(1)} %reshape.118), kind=kOutput, calls=%fused_computation.26 | convolution fusion | flops 1075314688 | bytes 6294528 | tf_op jit(solution)/shard_map/dot_general | solution.py:75
  305.3 1.4 slice.69
  306.7 44.7 %all-to-all-done.7 = bf16[64,64,256]{2,1,0:T(8,128)(2,1)S(1)} async-done(((bf16[64,64,256]{2,1,0:T(8,128)(2,1)}), bf16[64,64,256]{2,1,0:T(8,128)(2,1)S(1)}, u32[]{:S(2)}, u32[]{:S(2)}) %all-to-all-start.7) | async-done | bytes 2097184 | tf_op jit(solution)/shard_map/all_to_all | solution.py:106
  351.4 6.0 %all-to-all-start.5 = ((bf16[64,64,256]{2,1,0:T(8,128)(2,1)}), bf16[64,64,256]{2,1,0:T(8,128)(2,1)}, u32[]{:S(2)}, u32[]{:S(2)}) async-start(bf16[64,64,256]{2,1,0:T(8,128)(2,1)} %bitcast.67), calls=%async_computation.6 | async-start | bytes 4194304 | tf_op jit(solution)/shard_map/all_to_all | solution.py:106
  357.7 5.2 %add_multiply_fusion = f32[512,4,256]{2,0,1:T(8,128)} fusion(f32[512,4,256]{2,0,1:T(8,128)} %fusion.7, bf16[4,1152,256]{2,1,0:T(8,128)(2,1)} %all-to-all-done.1, bf16[1024,512]{1,0:T(8,128)(2,1)S(1)} %copy-done.8, bf16[128,512]{1,0:T(8,128)(2,1)S(1)} %fusion.10), kind=kOutput, calls=%fused_computation.20 | convolution fusion | flops 1211367424 | bytes 7733248 | tf_op jit(solution)/shard_map/dot_general | solution.py:75
  362.9 1.1 convert_add_fusion
  364.0 2.5 copy.35
  366.5 42.1 %all-to-all-done.5 = bf16[64,64,256]{2,1,0:T(8,128)(2,1)} async-done(((bf16[64,64,256]{2,1,0:T(8,128)(2,1)}), bf16[64,64,256]{2,1,0:T(8,128)(2,1)}, u32[]{:S(2)}, u32[]{:S(2)}) %all-to-all-start.5) | async-done | bytes 2097184 | tf_op jit(solution)/shard_map/all_to_all | solution.py:106
  408.6 2.8 copy.34
  411.4 0.7 fusion
  412.1 4.4 %copy.36 = f32[32,128,256]{2,1,0:T(8,128)} copy(f32[32,128,256]{2,0,1:T(8,128)S(1)} %fusion) | data formatting | bytes 8388608 | tf_op jit(solution)/shard_map/kr,rpd->kpd/dot_general | solution.py:114
  416.6 7.3 %scatter_fusion = f32[4096,256]{1,0:T(8,128)} fusion(f32[4096,256]{1,0:T(8,128)} %bitcast.65, s32[512]{0:T(512)S(1)} %compare_select_fusion, f32[512,256]{1,0:T(8,128)S(1)} %bitcast.71), kind=kCustom, calls=%fused_computation.2 | custom fusion | flops 131072 | bytes 1574912 | tf_op jit(solution)/shard_map/scatter-add | solution.py:115
  (49 shorter events, 1.8 us)
Async XLA Ops:
  7.2 2.1 copy-start
  136.6 4.6 %copy-start.9 = (bf16[512,256]{1,0:T(8,128)(2,1)S(1)}, bf16[512,256]{1,0:T(8,128)(2,1)}, u32[]{:S(2)}) copy-start(bf16[512,256]{1,0:T(8,128)(2,1)} %param.4) | copy-start | bytes 786436
  136.6 5.5 %copy-start.10 = (s32[512]{0:T(512)S(1)}, s32[512]{0:T(512)}, u32[]{:S(2)}) copy-start(s32[512]{0:T(512)} %param.6) | copy-start | bytes 6148
  136.6 39.1 %all-to-all-start.3 = ((bf16[4,1024,256]{2,1,0:T(8,128)(2,1)}), bf16[4,1024,256]{2,1,0:T(8,128)(2,1)}, u32[]{:S(2)}, u32[]{:S(2)}) async-start(bf16[4,1024,256]{2,1,0:T(8,128)(2,1)} %bitcast.68), calls=%async_computation.3 | async-start | bytes 4194304 | tf_op jit(solution)/shard_map/all_to_all | solution.py:42
  141.2 40.0 %all-gather.4.cloned.1.call-start = ((), (), s32[]{:S(2)}) async-start(), calls=%async_computation.9 | async-start | bytes 1310720 | tf_op jit(solution)/shard_map/all_gather | solution.py:27
  175.7 32.5 %all-to-all-start.1 = ((bf16[4,1152,256]{2,1,0:T(8,128)(2,1)}), bf16[4,1152,256]{2,1,0:T(8,128)(2,1)}, u32[]{:S(2)}, u32[]{:S(2)}) async-start(bf16[4,1152,256]{2,1,0:T(8,128)(2,1)} %pad_maximum_fusion.1), calls=%async_computation.1 | async-start | bytes 4718592 | tf_op jit(solution)/shard_map/all_to_all | solution.py:42
  184.4 38.5 %copy-start.5 = (f32[1024,512]{1,0:T(8,128)}, f32[1024,512]{1,0:T(8,128)S(1)}, u32[]{:S(2)}) copy-start(f32[1024,512]{1,0:T(8,128)S(1)} %get-tuple-element.20) | copy-start | bytes 6291460
  211.6 1.4 copy-start.2
  211.7 11.1 %copy-start.11 = (bf16[512,1024]{0,1:T(8,128)(2,1)S(1)}, bf16[512,1024]{0,1:T(8,128)(2,1)}, u32[]{:S(2)}) copy-start(bf16[512,1024]{0,1:T(8,128)(2,1)} %all-gather.4.cloned.1.call-done) | copy-start | bytes 3145732
  229.6 26.0 %all-to-all-start.6 = ((bf16[4,1024,256]{2,1,0:T(8,128)(2,1)}), bf16[4,1024,256]{2,1,0:T(8,128)(2,1)}, u32[]{:S(2)}, u32[]{:S(2)}) async-start(bf16[4,1024,256]{2,1,0:T(8,128)(2,1)} %bitcast.26), calls=%async_computation.7 | async-start | bytes 4194304 | tf_op jit(solution)/shard_map/all_to_all | solution.py:97
  236.4 1.6 copy-start.12
  236.5 1.0 copy-start.7
  239.5 2.8 copy-start.6
  286.2 65.3 %all-to-all-start.7 = ((bf16[64,64,256]{2,1,0:T(8,128)(2,1)}), bf16[64,64,256]{2,1,0:T(8,128)(2,1)S(1)}, u32[]{:S(2)}, u32[]{:S(2)}) async-start(bf16[64,64,256]{2,1,0:T(8,128)(2,1)} %bitcast.27), calls=%async_computation.8 | async-start | bytes 4194304 | tf_op jit(solution)/shard_map/all_to_all | solution.py:106
  300.2 5.1 %copy-start.3 = (bf16[4,1280,256]{2,1,0:T(8,128)(2,1)S(1)}, bf16[4,1280,256]{2,1,0:T(8,128)(2,1)}, u32[]{:S(2)}) copy-start(bf16[4,1280,256]{2,1,0:T(8,128)(2,1)} %all_to_all.42) | copy-start | bytes 7864324
  306.7 51.0 %copy-start.8 = (bf16[1024,512]{1,0:T(8,128)(2,1)S(1)}, bf16[1024,512]{1,0:T(8,128)(2,1)}, u32[]{:S(2)}) copy-start(bf16[1024,512]{1,0:T(8,128)(2,1)} %copy-done.7) | copy-start | bytes 3145732
  351.4 57.2 %all-to-all-start.5 = ((bf16[64,64,256]{2,1,0:T(8,128)(2,1)}), bf16[64,64,256]{2,1,0:T(8,128)(2,1)}, u32[]{:S(2)}, u32[]{:S(2)}) async-start(bf16[64,64,256]{2,1,0:T(8,128)(2,1)} %bitcast.67), calls=%async_computation.6 | async-start | bytes 4194304 | tf_op jit(solution)/shard_map/all_to_all | solution.py:106
  357.5 66.5 %reduce-scatter.2.cloned.1.call-start = ((), (), s32[]{:S(2)}) async-start(), calls=%async_computation.10 | async-start | bytes 2621440 | tf_op jit(solution)/shard_map/reduce_scatter | solution.py:79
  366.5 44.9 %copy-start.4 = (bf16[64,64,256]{2,0,1:T(8,128)(2,1)S(1)}, bf16[64,64,256]{2,0,1:T(8,128)(2,1)}, u32[]{:S(2)}) copy-start(bf16[64,64,256]{2,0,1:T(8,128)(2,1)} %copy.35) | copy-start | bytes 6291460
  416.6 7.3 %copy-start.1 = (bf16[4096,256]{1,0:T(8,128)(2,1)S(1)}, bf16[4096,256]{1,0:T(8,128)(2,1)}, u32[]{:S(2)}) copy-start(bf16[4096,256]{1,0:T(8,128)(2,1)} %param.5) | copy-start | bytes 6291460
Sparse Core Ops, SparseCore 0:
  144.4 30.5 all-gather.3
  363.0 31.3 reduce-scatter.1
where the time goes:
time: 432 us; the launch traced here: 431 us
  blocking collectives  161 us (37%)
  waiting for transfers between devices  146 us (34%)
  starting transfers between devices  34 us (8%)
  local copies, waits for them, and re-layouts  29.2 us (7%)
  other arithmetic  24 us (6%)
  matrix products  21.8 us (5%)
  between operations  14.4 us (3%)
    all_to_all x2, blocking collectives, body(): lax.all_to_all(outgoing[:, h * part:(h + 1) * part], 'dp', split_axis=0,...  121 us
    all_to_all x2, waiting for transfers between devices, body(): lax.all_to_all(sent.reshape(dp_count, part, shard_width), 'dp', split_axi...  86.8 us
    all_to_all x2, waiting for transfers between devices, body(): lax.all_to_all(send, 'mp', split_axis=0, concat_axis=0, tiled=True)  52.2 us
    all_to_all x1, blocking collectives, body(): lax.all_to_all(jnp.concatenate(pieces, axis=1), 'mp', split_axis=0, conca...  30.6 us
    all_to_all x2, starting transfers between devices, body(): lax.all_to_all(sent.reshape(dp_count, part, shard_width), 'dp', split_axi...  20 us
    dot_general x2, matrix products, body(): lax.dot_general(g, c, (((0,), (1,)), ((), ())), preferred_element_type=jn...  10.2 us
    all_gather x1, blocking collectives, body(): lax.all_gather(jnp.stack([local_top, local_total, local_own]), 'mp', axis=0)  9.14 us
    all_to_all x2, starting transfers between devices, body(): lax.all_to_all(send, 'mp', split_axis=0, concat_axis=0, tiled=True)  9.09 us
  transfers between devices with their start and end apart: 7, of which 5 were waited for; matrix products, arithmetic and copies ran while one was open for 12% of the time, Pallas kernels for 0%

commit v1 on v0

--- a/solution.py
+++ b/solution.py
@@ -1,3 +1,4 @@
+import functools
 import jax
 import jax.numpy as jnp
 from jax import lax
@@ -5,6 +6,45 @@
 
 PBS = 128
 HALVES = 2
+
+
+def try_all_units(piece_in, out_dim, packet):
+    carry_out = piece_in.shape
+    f_now = piece_in.reshape(
+        *carry_out[:out_dim], packet, carry_out[out_dim] // packet, *carry_out[out_dim + 1 :]
+    )
+    extra = jnp.moveaxis(f_now, out_dim, 0)
+    return extra
+
+
+def read_the_keys(work_x, ndim_at):
+    work_x = jnp.moveaxis(work_x, 0, ndim_at)
+    heard = work_x.shape
+    row_out = work_x.reshape(
+        *heard[:ndim_at], heard[ndim_at] * heard[ndim_at + 1], *heard[ndim_at + 2 :]
+    )
+    return row_out
+
+
+def chunk_treat(x_part, device_axis, original, matrix):
+    then, w_next = (lax.psum(1, axis_name=device_axis), lax.axis_index(device_axis))
+    known = try_all_units(x_part, original, then)
+    sides = [known[w_next]]
+    t = 1
+    while t < then:
+        o_now = known[w_next ^ t]
+        sides.append(
+            lax.ppermute(
+                o_now, axis_name=device_axis, perm=[(hop_no, hop_no ^ t) for hop_no in range(then)]
+            )
+        )
+        t += 1
+    known = jnp.stack(sides, 0)[w_next ^ jnp.arange(then)]
+    base_arr = read_the_keys(known, matrix)
+    return base_arr
+
+
+proceed_chains = functools.partial(chunk_treat, device_axis="mp", original=0, matrix=0)
 
 
 def body(queries, passages, positives, negatives):
@@ -39,7 +79,7 @@
                 [positive_rows.reshape(mp_count, pos_per, shard_width), send], axis=1
             )
             ok = jnp.concatenate([jnp.ones((pos_per,), bool), ok])
-        mine.append(lax.all_to_all(send, "mp", split_axis=0, concat_axis=0, tiled=True))
+        mine.append(proceed_chains(send))
         valid.append(ok)
     scores = [
         factor

time: 432 us -> 402 us (0.931)
  blocking collectives: 161 us -> 105 us
  local copies, waits for them, and re-layouts: 29.2 us -> 39 us
  waiting for transfers between devices: 146 us -> 155 us
    all_to_all x2 -> x1, blocking collectives: 121 us -> 64.3 us  [body(): lax.all_to_all(outgoing[:, h * part:(h + 1) * part], 'dp', split_axis=0,...]
    ppermute x0 -> x6, waiting for transfers between devices: none -> 18 us  [chunk_treat(): lax.ppermute(o_now, axis_name=device_axis, perm=[(hop_no, hop_no ^ t) for...]
    all_to_all x2 -> x1, waiting for transfers between devices: 52.2 us -> 42.3 us  [body(): lax.all_to_all(outgoing[:, h * part:(h + 1) * part], 'dp', split_axis=0,...]
    ppermute x0 -> x6, starting transfers between devices: none -> 6.51 us  [chunk_treat(): lax.ppermute(o_now, axis_name=device_axis, perm=[(hop_no, hop_no ^ t) for...]
    gather x0 -> x2, local copies, waits for them, and re-layouts: none -> 5.96 us  [chunk_treat(): known = jnp.stack(sides, 0)[w_next ^ jnp.arange(then)]]
    another operation x1 -> x3, other arithmetic: 0.1 us -> 4.84 us  [the longest x2 4.74 us: chunk_treat(): known = jnp.stack(sides, 0)[w_next ^ jnp.arange(then)]]
    all_to_all x2 -> x1, starting transfers between devices: 9.09 us -> 6.14 us  [body(): lax.all_to_all(outgoing[:, h * part:(h + 1) * part], 'dp', split_axis=0,...]
  transfers between devices with their start and end apart: 7 -> 12, of which waited for: 5 -> 6; matrix products, arithmetic and copies ran while one was open for 12% -> 15% of each run, Pallas kernels for 0% -> 0%
where the time goes in v1:
time: 402 us; the launch traced here: 400 us
  waiting for transfers between devices  155 us (39%)
  blocking collectives  105 us (26%)
  local copies, waits for them, and re-layouts  39 us (10%)
  starting transfers between devices  37.1 us (9%)
  other arithmetic  28.3 us (7%)
  matrix products  21.5 us (5%)
  between operations  14.4 us (4%)
    all_to_all x2, waiting for transfers between devices, body(): lax.all_to_all(sent.reshape(dp_count, part, shard_width), 'dp', split_axi...  86.8 us
    all_to_all x1, blocking collectives, body(): lax.all_to_all(outgoing[:, h * part:(h + 1) * part], 'dp', split_axis=0,...  64.3 us
    all_to_all x1, waiting for transfers between devices, body(): lax.all_to_all(outgoing[:, h * part:(h + 1) * part], 'dp', split_axis=0,...  42.3 us
    all_to_all x1, blocking collectives, body(): lax.all_to_all(jnp.concatenate(pieces, axis=1), 'mp', split_axis=0, conca...  31.2 us
    all_to_all x2, starting transfers between devices, body(): lax.all_to_all(sent.reshape(dp_count, part, shard_width), 'dp', split_axi...  19.8 us
    ppermute x6, waiting for transfers between devices, chunk_treat(): lax.ppermute(o_now, axis_name=device_axis, perm=[(hop_no, hop_no ^ t) for...  18 us
    dot_general x2, matrix products, body(): lax.dot_general(g, c, (((0,), (1,)), ((), ())), preferred_element_type=jn...  10.2 us
    all_gather x1, blocking collectives, body(): lax.all_gather(jnp.stack([local_top, local_total, local_own]), 'mp', axis=0)  9.56 us
  transfers between devices with their start and end apart: 12, of which 6 were waited for; matrix products, arithmetic and copies ran while one was open for 15% of the time, Pallas kernels for 0%

profile of v1, /device:TPU:1, one launch (start us, length us, event | category | flops | bytes accessed | tf_op | source)
XLA Modules:
  0.0 400.5 jit_solution(2275240063830343689)
XLA Ops:
  7.2 1.1 dynamic-slice_reduce_fusion
  8.3 0.9 compare_reduce_fusion
  9.3 2.8 gather_fusion.1
  12.1 2.7 select_select_fusion
  14.8 1.9 fusion.29
  16.6 64.3 %all_to_all.30 = bf16[64,64,256]{2,1,0:T(8,128)(2,1)} all-to-all(bf16[64,64,256]{2,1,0:T(8,128)(2,1)S(1)} %get-tuple-element.11), channel_id=1, replica_groups=mesh['dp'=64,'mp'=4] {'dp'}, dimensions={0} | all-to-all | bytes 4194304 | tf_op jit(solution)/shard_map/all_to_all | solution.py:72
  80.9 6.1 %all-to-all-start = ((bf16[64,64,256]{2,1,0:T(8,128)(2,1)}), bf16[64,64,256]{2,1,0:T(8,128)(2,1)}, u32[]{:S(2)}, u32[]{:S(2)}) async-start(bf16[64,64,256]{2,1,0:T(8,128)(2,1)} %get-tuple-element.12), calls=%async_computation | async-start | bytes 4194304 | tf_op jit(solution)/shard_map/all_to_all | solution.py:72
  87.1 0.9 copy.24
  88.1 2.0 gather_fusion
  90.2 2.5 constant_dynamic-slice_fusion
  92.7 2.5 collective-permute-start.5
  95.9 42.3 %all-to-all-done = bf16[64,64,256]{2,1,0:T(8,128)(2,1)} async-done(((bf16[64,64,256]{2,1,0:T(8,128)(2,1)}), bf16[64,64,256]{2,1,0:T(8,128)(2,1)}, u32[]{:S(2)}, u32[]{:S(2)}) %all-to-all-start) | async-done | bytes 2097184 | tf_op jit(solution)/shard_map/all_to_all | solution.py:72
  138.2 2.8 fusion.11
  141.0 2.5 collective-permute-start.2
  144.3 0.8 compare_bitcast_fusion
  145.2 1.6 maximum_bitcast_fusion.1
  146.8 2.1 gather_fusion.3
  148.9 3.1 fusion.31
  152.1 17.6 %collective-permute-done.2 = bf16[1,1152,256]{2,1,0:T(8,128)(2,1)} collective-permute-done((bf16[1,1152,256]{2,1,0:T(8,128)(2,1)}, bf16[1,1152,256]{2,1,0:T(8,128)(2,1)}, u32[]{:S(2)}, u32[]{:S(2)}) %collective-permute-start.2) | collective-permute-done | bytes 589856 | tf_op jit(solution)/shard_map/ppermute | solution.py:37
  170.0 3.1 maximum_bitcast_fusion
  173.1 3.9 gather_fusion.2
  177.0 3.1 select_reduce_fusion.2
  181.5 9.6 %all-gather.1 = f32[4,3,512]{2,1,0:T(4,128)S(1)} all-gather(f32[1,3,512]{2,1,0:T(4,128)S(1)} %maximum_bitcast_fusion.2), channel_id=2, replica_groups=mesh['dp'=64,'mp'=4] {'mp'}, dimensions={0}, use_global_device_ids=true | all-gather | bytes 30720 | tf_op jit(solution)/shard_map/all_gather | solution.py:101
  191.8 2.8 multiply_convert_fusion
  194.6 3.9 copy.33
  198.5 4.4 %all-to-all-start.4 = ((bf16[4,1024,256]{2,1,0:T(8,128)(2,1)}), bf16[4,1024,256]{2,1,0:T(8,128)(2,1)}, u32[]{:S(2)}, u32[]{:S(2)}) async-start(bf16[4,1024,256]{2,1,0:T(8,128)(2,1)} %bitcast.39), calls=%async_computation.5 | async-start | bytes 4194304 | tf_op jit(solution)/shard_map/all_to_all | solution.py:137
  203.0 2.1 exponential_select_fusion
  205.4 0.9 copy-done.7
  206.7 1.6 convolution_multiply_fusion
  208.3 1.9 slice.90
  210.2 0.9 copy-done.6
  211.1 2.8 copy.32
  213.9 1.1 reduce-precision_convert_fusion
  215.3 1.7 pad_maximum_fusion
  217.0 8.0 %all-to-all-done.4 = bf16[4,1024,256]{2,1,0:T(8,128)(2,1)} async-done(((bf16[4,1024,256]{2,1,0:T(8,128)(2,1)}), bf16[4,1024,256]{2,1,0:T(8,128)(2,1)}, u32[]{:S(2)}, u32[]{:S(2)}) %all-to-all-start.4) | async-done | bytes 2097184 | tf_op jit(solution)/shard_map/all_to_all | solution.py:137
  225.0 31.2 %all_to_all.31 = bf16[4,1280,256]{2,1,0:T(8,128)(2,1)} all-to-all(bf16[4,1280,256]{2,1,0:T(8,128)(2,1)} %pad_maximum_fusion), channel_id=1, replica_groups=mesh['dp'=64,'mp'=4] {'mp'}, dimensions={0} | all-to-all | bytes 5242880 | tf_op jit(solution)/shard_map/all_to_all | solution.py:137
  256.1 13.7 %all-to-all-start.5 = ((bf16[64,64,256]{2,1,0:T(8,128)(2,1)}), bf16[64,64,256]{2,1,0:T(8,128)(2,1)S(1)}, u32[]{:S(2)}, u32[]{:S(2)}) async-start(bf16[64,64,256]{2,1,0:T(8,128)(2,1)} %bitcast.40), calls=%async_computation.6 | async-start | bytes 4194304 | tf_op jit(solution)/shard_map/all_to_all | solution.py:146
  269.9 5.1 %fusion.7 = f32[512,4,256]{2,0,1:T(8,128)} fusion(bf16[4,1024,256]{2,1,0:T(8,128)(2,1)} %gather_fusion.3, f32[1024,512]{1,0:T(8,128)} %copy-done.5, f32[512]{0:T(512)S(1)} %get-tuple-element.8, pred[1024]{0:T(1024)(128)(4,1)S(1)} %reshape.145), kind=kOutput, calls=%fused_computation.37 | convolution fusion | flops 1075314688 | bytes 6294528 | tf_op jit(solution)/shard_map/dot_general | solution.py:115
  275.0 1.5 slice.73
  276.5 44.7 %all-to-all-done.5 = bf16[64,64,256]{2,1,0:T(8,128)(2,1)S(1)} async-done(((bf16[64,64,256]{2,1,0:T(8,128)(2,1)}), bf16[64,64,256]{2,1,0:T(8,128)(2,1)S(1)}, u32[]{:S(2)}, u32[]{:S(2)}) %all-to-all-start.5) | async-done | bytes 2097184 | tf_op jit(solution)/shard_map/all_to_all | solution.py:146
  321.1 6.0 %all-to-all-start.3 = ((bf16[64,64,256]{2,1,0:T(8,128)(2,1)}), bf16[64,64,256]{2,1,0:T(8,128)(2,1)}, u32[]{:S(2)}, u32[]{:S(2)}) async-start(bf16[64,64,256]{2,1,0:T(8,128)(2,1)} %bitcast.87), calls=%async_computation.4 | async-start | bytes 4194304 | tf_op jit(solution)/shard_map/all_to_all | solution.py:146
  327.4 5.2 %add_multiply_fusion = f32[512,4,256]{2,0,1:T(8,128)} fusion(f32[512,4,256]{2,0,1:T(8,128)} %fusion.7, bf16[4,1152,256]{2,1,0:T(8,128)(2,1)} %gather_fusion.2, bf16[1024,512]{1,0:T(8,128)(2,1)S(1)} %copy-done.8, bf16[128,512]{1,0:T(8,128)(2,1)S(1)} %fusion.15), kind=kOutput, calls=%fused_computation.27 | convolution fusion | flops 1211367424 | bytes 7733248 | tf_op jit(solution)/shard_map/dot_general | solution.py:115
  332.6 1.1 convert_add_fusion
  333.7 2.5 copy.35
  336.2 42.1 %all-to-all-done.3 = bf16[64,64,256]{2,1,0:T(8,128)(2,1)} async-done(((bf16[64,64,256]{2,1,0:T(8,128)(2,1)}), bf16[64,64,256]{2,1,0:T(8,128)(2,1)}, u32[]{:S(2)}, u32[]{:S(2)}) %all-to-all-start.3) | async-done | bytes 2097184 | tf_op jit(solution)/shard_map/all_to_all | solution.py:146
  378.3 2.8 copy.34
  381.8 4.4 %copy.36 = f32[32,128,256]{2,1,0:T(8,128)} copy(f32[32,128,256]{2,0,1:T(8,128)S(1)} %fusion) | data formatting | bytes 8388608 | tf_op jit(solution)/shard_map/kr,rpd->kpd/dot_general | solution.py:154
  386.3 7.3 %scatter_fusion = f32[4096,256]{1,0:T(8,128)} fusion(f32[4096,256]{1,0:T(8,128)} %bitcast.85, s32[512]{0:T(512)S(1)} %compare_select_fusion, f32[512,256]{1,0:T(8,128)S(1)} %bitcast.90), kind=kCustom, calls=%fused_computation.4 | custom fusion | flops 131072 | bytes 1574912 | tf_op jit(solution)/shard_map/scatter-add | solution.py:155
  (69 shorter events, 6.4 us)
Async XLA Ops:
  7.2 2.1 copy-start
  80.9 6.2 %copy-start.10 = (bf16[512,256]{1,0:T(8,128)(2,1)S(1)}, bf16[512,256]{1,0:T(8,128)(2,1)}, u32[]{:S(2)}) copy-start(bf16[512,256]{1,0:T(8,128)(2,1)} %param.4) | copy-start | bytes 786436
  80.9 7.1 %copy-start.11 = (s32[512]{0:T(512)S(1)}, s32[512]{0:T(512)}, u32[]{:S(2)}) copy-start(s32[512]{0:T(512)} %param.6) | copy-start | bytes 6148
  80.9 57.3 %all-to-all-start = ((bf16[64,64,256]{2,1,0:T(8,128)(2,1)}), bf16[64,64,256]{2,1,0:T(8,128)(2,1)}, u32[]{:S(2)}, u32[]{:S(2)}) async-start(bf16[64,64,256]{2,1,0:T(8,128)(2,1)} %get-tuple-element.12), calls=%async_computation | async-start | bytes 4194304 | tf_op jit(solution)/shard_map/all_to_all | solution.py:72
  87.1 61.8 %all-gather.4.cloned.1.call-start = ((), (), s32[]{:S(2)}) async-start(), calls=%async_computation.7 | async-start | bytes 1310720 | tf_op jit(solution)/shard_map/all_gather | solution.py:67
  92.7 51.3 %collective-permute-start.5 = (bf16[1,1024,256]{2,1,0:T(8,128)(2,1)}, bf16[1,1024,256]{2,1,0:T(8,128)(2,1)S(1)}, u32[]{:S(2)}, u32[]{:S(2)}) collective-permute-start(bf16[1,1024,256]{2,1,0:T(8,128)(2,1)} %get-tuple-element.18), channel_id=1, source_target_pairs={{0,3},{1,2},{2,1},{3,0},{4,7},{5,6},{6,5},{7,4},{8,11},{9,10},{10,... | collective-permute-start | bytes 1572872 | tf_op jit(solution)/shard_map/ppermute | solution.py:37
  95.2 50.0 %collective-permute-start.4 = (bf16[1,1024,256]{2,1,0:T(8,128)(2,1)S(1)}, bf16[1,1024,256]{2,1,0:T(8,128)(2,1)}, u32[]{:S(2)}, u32[]{:S(2)}) collective-permute-start(bf16[1,1024,256]{2,1,0:T(8,128)(2,1)S(1)} %get-tuple-element.19), channel_id=1, source_target_pairs={{0,2},{1,3},{2,0},{3,1},{4,6},{5,7},{6,4},{7,5},{8,10},{9,11},{10,... | collective-permute-start | bytes 1572872 | tf_op jit(solution)/shard_map/ppermute | solution.py:37
  95.7 49.5 %collective-permute-start.3 = (bf16[1,1024,256]{2,1,0:T(8,128)(2,1)S(1)}, bf16[1,1024,256]{2,1,0:T(8,128)(2,1)}, u32[]{:S(2)}, u32[]{:S(2)}) collective-permute-start(bf16[1,1024,256]{2,1,0:T(8,128)(2,1)S(1)} %get-tuple-element.20), channel_id=1, source_target_pairs={{0,1},{1,0},{2,3},{3,2},{4,5},{5,4},{6,7},{7,6},{8,9},{9,8},{10,11... | collective-permute-start | bytes 1572872 | tf_op jit(solution)/shard_map/ppermute | solution.py:37
  141.0 28.7 %collective-permute-start.2 = (bf16[1,1152,256]{2,1,0:T(8,128)(2,1)}, bf16[1,1152,256]{2,1,0:T(8,128)(2,1)}, u32[]{:S(2)}, u32[]{:S(2)}) collective-permute-start(bf16[1,1152,256]{2,1,0:T(8,128)(2,1)} %get-tuple-element.16), channel_id=1, source_target_pairs={{0,3},{1,2},{2,1},{3,0},{4,7},{5,6},{6,5},{7,4},{8,11},{9,10},{10,... | collective-permute-start | bytes 1769480 | tf_op jit(solution)/shard_map/ppermute | solution.py:37
  143.5 26.2 %collective-permute-start.1 = (bf16[1,1152,256]{2,1,0:T(8,128)(2,1)}, bf16[1,1152,256]{2,1,0:T(8,128)(2,1)}, u32[]{:S(2)}, u32[]{:S(2)}) collective-permute-start(bf16[1,1152,256]{2,1,0:T(8,128)(2,1)} %get-tuple-element.15), channel_id=1, source_target_pairs={{0,2},{1,3},{2,0},{3,1},{4,6},{5,7},{6,4},{7,5},{8,10},{9,11},{10,... | collective-permute-start | bytes 1769480 | tf_op jit(solution)/shard_map/ppermute | solution.py:37
  144.0 1.2 copy-start.9
  144.0 26.0 %collective-permute-start = (bf16[1,1152,256]{2,1,0:T(8,128)(2,1)}, bf16[1,1152,256]{2,1,0:T(8,128)(2,1)}, u32[]{:S(2)}, u32[]{:S(2)}) collective-permute-start(bf16[1,1152,256]{2,1,0:T(8,128)(2,1)} %get-tuple-element.14), channel_id=1, source_target_pairs={{0,1},{1,0},{2,3},{3,2},{4,5},{5,4},{6,7},{7,6},{8,9},{9,8},{10,11... | collective-permute-start | bytes 1769480 | tf_op jit(solution)/shard_map/ppermute | solution.py:37
  152.0 39.7 %copy-start.5 = (f32[1024,512]{1,0:T(8,128)}, f32[1024,512]{1,0:T(8,128)S(1)}, u32[]{:S(2)}) copy-start(f32[1024,512]{1,0:T(8,128)S(1)} %get-tuple-element.28) | copy-start | bytes 6291460
  173.1 3.9 copy-start.12
  180.1 1.4 copy-start.2
  180.2 11.5 %copy-start.13 = (bf16[512,1024]{0,1:T(8,128)(2,1)S(1)}, bf16[512,1024]{0,1:T(8,128)(2,1)}, u32[]{:S(2)}) copy-start(bf16[512,1024]{0,1:T(8,128)(2,1)} %all-gather.4.cloned.1.call-done) | copy-start | bytes 3145732
  198.5 26.5 %all-to-all-start.4 = ((bf16[4,1024,256]{2,1,0:T(8,128)(2,1)}), bf16[4,1024,256]{2,1,0:T(8,128)(2,1)}, u32[]{:S(2)}, u32[]{:S(2)}) async-start(bf16[4,1024,256]{2,1,0:T(8,128)(2,1)} %bitcast.39), calls=%async_computation.5 | async-start | bytes 4194304 | tf_op jit(solution)/shard_map/all_to_all | solution.py:137
  205.1 1.6 copy-start.14
  205.3 1.0 copy-start.7
  208.3 2.8 copy-start.6
  256.1 65.0 %all-to-all-start.5 = ((bf16[64,64,256]{2,1,0:T(8,128)(2,1)}), bf16[64,64,256]{2,1,0:T(8,128)(2,1)S(1)}, u32[]{:S(2)}, u32[]{:S(2)}) async-start(bf16[64,64,256]{2,1,0:T(8,128)(2,1)} %bitcast.40), calls=%async_computation.6 | async-start | bytes 4194304 | tf_op jit(solution)/shard_map/all_to_all | solution.py:146
  269.9 5.1 %copy-start.3 = (bf16[4,1280,256]{2,1,0:T(8,128)(2,1)S(1)}, bf16[4,1280,256]{2,1,0:T(8,128)(2,1)}, u32[]{:S(2)}) copy-start(bf16[4,1280,256]{2,1,0:T(8,128)(2,1)} %all_to_all.31) | copy-start | bytes 7864324
  276.4 51.0 %copy-start.8 = (bf16[1024,512]{1,0:T(8,128)(2,1)S(1)}, bf16[1024,512]{1,0:T(8,128)(2,1)}, u32[]{:S(2)}) copy-start(bf16[1024,512]{1,0:T(8,128)(2,1)} %copy-done.7) | copy-start | bytes 3145732
  321.1 57.2 %all-to-all-start.3 = ((bf16[64,64,256]{2,1,0:T(8,128)(2,1)}), bf16[64,64,256]{2,1,0:T(8,128)(2,1)}, u32[]{:S(2)}, u32[]{:S(2)}) async-start(bf16[64,64,256]{2,1,0:T(8,128)(2,1)} %bitcast.87), calls=%async_computation.4 | async-start | bytes 4194304 | tf_op jit(solution)/shard_map/all_to_all | solution.py:146
  327.2 66.4 %reduce-scatter.2.cloned.1.call-start = ((), (), s32[]{:S(2)}) async-start(), calls=%async_computation.8 | async-start | bytes 2621440 | tf_op jit(solution)/shard_map/reduce_scatter | solution.py:119
  336.2 44.9 %copy-start.4 = (bf16[64,64,256]{2,0,1:T(8,128)(2,1)S(1)}, bf16[64,64,256]{2,0,1:T(8,128)(2,1)}, u32[]{:S(2)}) copy-start(bf16[64,64,256]{2,0,1:T(8,128)(2,1)} %copy.35) | copy-start | bytes 6291460
  386.3 7.3 %copy-start.1 = (bf16[4096,256]{1,0:T(8,128)(2,1)S(1)}, bf16[4096,256]{1,0:T(8,128)(2,1)}, u32[]{:S(2)}) copy-start(bf16[4096,256]{1,0:T(8,128)(2,1)} %param.5) | copy-start | bytes 6291460
Sparse Core Ops, SparseCore 0:
  89.7 37.7 all-gather.3
  332.8 31.3 reduce-scatter.1
